TPU v7x, 128 devices: a whole 4x4x4 slice. The times are simulated.
128 devices in a mesh: leaf: 8 (over z, core), expert: 8 (over x_hi, y), tensor: 2 (over x_lo).
Axes of the slice: x: 4 (x_hi: 2, x_lo: 2; x = x_hi * 2 + x_lo), y: 4, z: 4, core: 2. Of those that a mesh axis runs over, the one named last changes fastest.
Arguments:
- drafts: bfloat16 [2048, 6144], P('leaf', ('expert', 'tensor')), may hold values from -6 to 6
- children: bfloat16 [4096, 6144], P('leaf', ('expert', 'tensor')), may hold values from -6 to 6
- child_order: int32 [16], replicated, may hold values from 0 to 15, each once
- spans: int32 [4096], P('leaf'), may hold values from 0 to 15
- span_bias: float32 [48, 16], P(('expert', 'tensor')), may hold values from -4 to 4
- out_weight: bfloat16 [6144, 6144], P(('expert', 'tensor')), may hold values from -0.078125 to 0.078125
- norm_gain: float32 [6144], replicated, may hold values from 0.1 to 1.9
- router: bfloat16 [6144, 8], replicated, may hold values from -0.078125 to 0.078125
- routes: int32 [2048, 2], P(('leaf', 'expert')), may hold values from 0 to 7, all different within a row; in each aligned block of 32 rows (0 to 31, 32 to 63, ...) at most 16 rows name the same one
- w_gate: bfloat16 [8, 6144, 8192], P('expert', None, ('leaf', 'tensor')), may hold values from -0.078125 to 0.078125
- w_up: bfloat16 [8, 6144, 8192], P('expert', None, ('leaf', 'tensor')), may hold values from -0.078125 to 0.078125
- w_down: bfloat16 [8, 8192, 6144], P('expert', ('leaf', 'tensor')), may hold values from -0.0625 to 0.0625
Outputs:
- merged_out: float32 [2048, 6144], P(('leaf', 'expert'))
Inputs may be any that keep to these rules, and one draw needn't show every extreme that they name: `routes`: each row names two different experts; within the rows of one index pair of leaf and expert (32 aligned rows) no expert is named more than 16 times, and exactly 16 times in some of them. `child_order`: A permutation: every parent has exactly two children.
All inputs are finite; a program needn't handle non-finite values.
Results may differ from a plain program's by a relative error of at most 0.013.
Values may be sent and summed in bfloat16 or wider, within the bound.
No kernel may reach another device: no remote copies, remote signals or barrier semaphores. Data moves between devices by JAX's collectives and lax.ppermute only.
A program may use at most 128 MiB of HBM per device.

v0:
```python
import math
import jax
import jax.numpy as jnp
from jax import lax
from jax.sharding import PartitionSpec as P

R = 256


def attend_parent(queries, keys, key_spans, span_bias, scale):
    rows, local_width = queries.shape
    heads_here, span_count = span_bias.shape
    head_size = local_width // heads_here
    key_count = keys.shape[0]
    q = queries.reshape(rows, heads_here, head_size)
    k = keys.reshape(key_count, heads_here, head_size)
    scores = jnp.einsum("qhd,khd->hqk", q, k, preferred_element_type=jnp.float32) * scale
    span_hot = (key_spans[:, None] == jnp.arange(span_count, dtype=jnp.int32)[None, :]).astype(
        jnp.float32
    )
    bias = jnp.dot(span_hot, span_bias.T, precision=lax.Precision.HIGHEST)
    scores = scores + bias.T[:, None, :]
    top = jnp.max(scores, axis=-1, keepdims=True)
    weights = jnp.exp(scores - top)
    total = jnp.sum(weights, axis=-1, keepdims=True)
    high = weights.astype(jnp.bfloat16)
    low = (weights - high.astype(jnp.float32)).astype(jnp.bfloat16)
    values = jnp.einsum("hqk,khd->hqd", high, k, preferred_element_type=jnp.float32) + jnp.einsum(
        "hqk,khd->hqd", low, k, preferred_element_type=jnp.float32
    )
    return (values / total).transpose(1, 0, 2).reshape(rows, local_width).astype(jnp.bfloat16)


def pair_gather(share):
    other = lax.ppermute(share, "tensor", perm=[(0, 1), (1, 0)])
    low = lax.axis_index("tensor") == 0
    return jnp.concatenate([jnp.where(low, share, other), jnp.where(low, other, share)], axis=0)


def per_device(
    drafts,
    children,
    child_order,
    spans,
    span_bias,
    out_weight,
    norm_gain,
    router,
    routes,
    w_gate,
    w_up,
    w_down,
):
    local_rows, local_width = drafts.shape
    heads_here = span_bias.shape[0]
    head_size = local_width // heads_here
    width = out_weight.shape[1]
    scale = 1.0 / math.sqrt(head_size)
    parents_here = local_rows // R
    leaf_index = lax.axis_index("leaf")
    child_rows = children.shape[0]
    children_here = child_rows // R
    span_rows = -(-spans.shape[0] // local_width)
    span_rows = -(-span_rows // 8) * 8
    span_block = jnp.pad(spans.astype(jnp.bfloat16), (0, span_rows * local_width - spans.shape[0]))
    payload = jnp.concatenate([children, span_block.reshape(span_rows, local_width)], axis=0)
    n_leaf = lax.axis_size("leaf")
    n_z = n_leaf // 2
    core = leaf_index % 2
    z = leaf_index // 2
    got = [payload]
    for k in range(1, n_z):
        perm = [(a * 2 + b, (a + k) % n_z * 2 + b) for a in range(n_z) for b in range(2)]
        got.append(lax.ppermute(payload, "leaf", perm=perm))
    swap = [(j, j ^ 1) for j in range(n_leaf)]
    got = got + [lax.ppermute(block, "leaf", perm=swap) for block in got]
    gathered = jnp.stack(got)
    span_table = gathered[:, child_rows:].reshape(gathered.shape[0], span_rows * local_width)
    count = child_order.shape[0]
    ids = jnp.arange(count, dtype=jnp.int32)
    inverse = jnp.sum(jnp.where(child_order[None, :] == ids[:, None], ids[None, :], 0), axis=1)

    def child_keys(child):
        owner = child // children_here
        slot = jnp.where(owner % 2 == core, 0, n_z) + (z - owner // 2) % n_z
        offset = child % children_here * R
        rows = lax.dynamic_slice(gathered, (slot, offset, 0), (1, R, local_width))[0]
        marks = lax.dynamic_slice(span_table, (slot, offset), (1, R))[0]
        return (rows, marks.astype(jnp.int32))

    pieces = []
    for i in range(parents_here):
        parent = leaf_index * parents_here + i
        first_rows, first_spans = child_keys(inverse[2 * parent])
        second_rows, second_spans = child_keys(inverse[2 * parent + 1])
        own_keys = jnp.concatenate([first_rows, second_rows], axis=0)
        own_spans = jnp.concatenate([first_spans, second_spans], axis=0)
        pieces.append(
            attend_parent(drafts[i * R : (i + 1) * R], own_keys, own_spans, span_bias, scale)
        )
    attended = pieces[0] if parents_here == 1 else jnp.concatenate(pieces, axis=0)
    term = jnp.dot(attended, out_weight, preferred_element_type=jnp.float32)
    offset = lax.axis_index(("expert", "tensor")) * local_width
    own_cols = lax.dynamic_slice(term, (0, offset), (local_rows, local_width)) + drafts.astype(
        jnp.float32
    )
    term = lax.dynamic_update_slice(term, own_cols, (0, offset)).astype(jnp.bfloat16)
    group = lax.axis_size(("expert", "tensor"))
    share_rows = local_rows // group
    arrived_terms = lax.all_to_all(
        term.reshape(group, share_rows, width), ("expert", "tensor"), 0, 0, tiled=True
    )
    share = jnp.sum(arrived_terms.astype(jnp.float32), axis=0)
    mean_square = jnp.mean(share * share, axis=-1, keepdims=True)
    normed = pair_gather((share * lax.rsqrt(mean_square + 1e-05) * norm_gain).astype(jnp.bfloat16))
    logits = jnp.dot(normed, router, preferred_element_type=jnp.float32)
    experts = router.shape[1]
    tok_count = routes.shape[0]
    capacity = 4 * tok_count // lax.axis_size("expert")
    choice_hot = routes[:, :, None] == jnp.arange(experts, dtype=jnp.int32)[None, None, :]
    chosen = jnp.sum(jnp.where(choice_hot, logits[:, None, :], 0.0), axis=-1)
    gates = jax.nn.softmax(chosen, axis=-1)
    pairs = routes.reshape(-1)
    pair_hot = (pairs[:, None] == jnp.arange(experts, dtype=jnp.int32)[None, :]).astype(jnp.int32)
    earlier = jnp.cumsum(pair_hot, axis=0) - pair_hot
    slot_index = jnp.sum(earlier * pair_hot, axis=1)
    target = pairs * capacity + slot_index
    place_hot = (
        jnp.arange(experts * capacity, dtype=jnp.int32)[:, None] == target[None, :]
    ).astype(jnp.bfloat16)
    place_rows = jnp.sum(place_hot.reshape(experts * capacity, tok_count, 2), axis=-1)
    outgoing = jnp.dot(place_rows, normed, preferred_element_type=jnp.float32).astype(jnp.bfloat16)
    outgoing = outgoing.reshape(experts, capacity, width)
    chunks = 2
    chunk_slots = capacity // chunks
    returned = []
    for c in range(chunks):
        arrived = lax.all_to_all(
            outgoing[:, c * chunk_slots : (c + 1) * chunk_slots],
            "expert",
            split_axis=0,
            concat_axis=0,
            tiled=True,
        ).reshape(-1, width)
        piece = lax.all_gather(arrived, "leaf", axis=0, tiled=True)
        if c == 0:
            piece, share = lax.optimization_barrier((piece, share))
            other_share = lax.ppermute(share, "tensor", perm=[(0, 1), (1, 0)])
        else:
            piece, other_share = lax.optimization_barrier((piece, other_share))
        gate_v = jnp.dot(piece, w_gate[0], preferred_element_type=jnp.float32)
        up_v = jnp.dot(piece, w_up[0], preferred_element_type=jnp.float32)
        hidden = (jax.nn.silu(gate_v) * up_v).astype(jnp.bfloat16)
        down = jnp.dot(hidden, w_down[0], preferred_element_type=jnp.float32).astype(jnp.bfloat16)
        part_rows = lax.psum_scatter(down, "leaf", scatter_dimension=0, tiled=True)
        returned.append(
            lax.all_to_all(
                part_rows.reshape(experts, chunk_slots, width),
                "expert",
                split_axis=0,
                concat_axis=0,
                tiled=True,
            )
        )
    back = jnp.concatenate(returned, axis=1).reshape(-1, width)
    low = lax.axis_index("tensor") == 0
    merged = jnp.concatenate(
        [jnp.where(low, share, other_share), jnp.where(low, other_share, share)], axis=0
    )
    picked = jnp.take(back, target, axis=0)
    picked = picked.astype(jnp.float32).reshape(tok_count, 2, width)
    own_mix = (gates[:, 0:1] * picked[:, 0] + gates[:, 1:2] * picked[:, 1]).astype(jnp.bfloat16)
    other_mix = lax.ppermute(own_mix, "tensor", perm=[(0, 1), (1, 0)])
    mixed = own_mix.astype(jnp.float32) + other_mix.astype(jnp.float32)
    return merged + mixed


def solution(mesh):
    in_specs = (
        P("leaf", ("expert", "tensor")),
        P("leaf", ("expert", "tensor")),
        P(),
        P("leaf"),
        P(("expert", "tensor"), None),
        P(("expert", "tensor"), None),
        P(),
        P(),
        P(("leaf", "expert"), None),
        P("expert", None, ("leaf", "tensor")),
        P("expert", None, ("leaf", "tensor")),
        P("expert", ("leaf", "tensor"), None),
    )
    out_specs = P(("leaf", "expert"), None)
    return jax.shard_map(
        per_device, mesh=mesh, in_specs=in_specs, out_specs=out_specs, check_vma=False
    )
```

profile of v0, /device:TPU:32, one launch (start us, length us, event | category | flops | bytes accessed | tf_op | source)
XLA Modules:
  0.0 337.6 jit_solution(6291394186603698562)
XLA Ops:
  6.5 1.2 copy.74
  8.7 2.0 collective-permute-start
  10.7 1.2 collective-permute-start.1
  11.8 2.5 collective-permute-start.2
  21.9 9.8 %collective-permute-done = bf16[520,384]{0,1:T(8,128)(2,1)S(1)} collective-permute-done((bf16[520,384]{0,1:T(8,128)(2,1)S(1)}, bf16[520,384]{0,1:T(8,128)(2,1)S(1)}, u32[]{:S(2)}, u32[]{:S(2)}) %collective-permute-start) | collective-permute-done | bytes 399392 | tf_op jit(solution)/shard_map/ppermute | solution.py:74
  32.3 2.7 collective-permute-done.2
  35.4 1.5 collective-permute-done.6
  41.0 1.8 fusion.50
  42.9 2.1 convert_element_type.89
  45.0 7.2 %all-to-all-start = ((bf16[16,16,6144]{2,1,0:T(8,128)(2,1)}), bf16[16,16,6144]{2,1,0:T(8,128)(2,1)S(1)}, u32[]{:S(2)}, u32[]{:S(2)}) async-start(bf16[16,16,6144]{2,1,0:T(8,128)(2,1)} %bitcast.114), calls=%async_computation | async-start | bytes 6291456 | tf_op jit(solution)/shard_map/all_to_all | solution.py:110
  52.9 45.7 %all-to-all-done = bf16[16,16,6144]{2,1,0:T(8,128)(2,1)S(1)} async-done(((bf16[16,16,6144]{2,1,0:T(8,128)(2,1)}), bf16[16,16,6144]{2,1,0:T(8,128)(2,1)S(1)}, u32[]{:S(2)}, u32[]{:S(2)}) %all-to-all-start) | async-done | bytes 3145760 | tf_op jit(solution)/shard_map/all_to_all | solution.py:110
  100.0 2.8 collective-permute-start.7
  102.8 4.0 %collective-permute-done.7 = bf16[16,6144]{1,0:T(8,128)(2,1)S(1)} collective-permute-done((bf16[16,6144]{1,0:T(8,128)(2,1)S(1)}, bf16[16,6144]{1,0:T(8,128)(2,1)S(1)}, u32[]{:S(2)}, u32[]{:S(2)}) %collective-permute-start.7) | collective-permute-done | bytes 196640 | tf_op jit(solution)/shard_map/ppermute | solution.py:35
  106.8 1.2 broadcast_select_fusion.3
  108.7 17.8 %all_to_all.25 = bf16[8,8,6144]{2,1,0:T(8,128)(2,1)} all-to-all(bf16[8,8,6144]{2,1,0:T(8,128)(2,1)S(1)} %get-tuple-element.19), channel_id=1, replica_groups=mesh['leaf'=8,'expert'=8,'tensor'=2] {'expert'}, dimensions={0} | all-to-all | bytes 1572864 | tf_op jit(solution)/shard_map/all_to_all | solution.py:138
  126.6 14.6 %all_to_all.26 = bf16[8,8,6144]{2,1,0:T(8,128)(2,1)} all-to-all(bf16[8,8,6144]{2,1,0:T(8,128)(2,1)S(1)} %get-tuple-element.20), channel_id=1, replica_groups=mesh['leaf'=8,'expert'=8,'tensor'=2] {'expert'}, dimensions={0} | all-to-all | bytes 1572864 | tf_op jit(solution)/shard_map/all_to_all | solution.py:138
  141.5 22.4 %all-gather.3.cloned.1.call-done = bf16[512,6144]{1,0:T(8,128)(2,1)} async-done(((bf16[64,6144]{1,0:T(8,128)(2,1)}), bf16[512,6144]{1,0:T(8,128)(2,1)}) %all-gather.3.cloned.1.call-update) | async-done | bytes 6291472 | tf_op jit(solution)/shard_map/all_gather | solution.py:145
  163.9 8.2 %fusion.8 = f32[512,512]{1,0:T(8,128)S(1)} fusion(bf16[512,6144]{1,0:T(8,128)(2,1)} %all-gather.3.cloned.1.call-done, bf16[1,6144,512]{2,1,0:T(8,128)(2,1)} %param.21), kind=kOutput, calls=%fused_computation.12 | convolution fusion | flops 3221225472 | bytes 13631488 | tf_op jit(solution)/shard_map/dot_general | solution.py:151
  172.2 6.4 %fusion.14 = bf16[512,512]{1,0:T(8,128)(2,1)S(1)} fusion(bf16[512,6144]{1,0:T(8,128)(2,1)S(1)} %copy-done.7, bf16[1,6144,512]{2,1,0:T(8,128)(2,1)} %param.22, f32[512,512]{1,0:T(8,128)S(1)} %fusion.8), kind=kOutput, calls=%fused_computation.22 | convolution fusion | flops 3222798336 | bytes 14155776 | tf_op jit(solution)/shard_map/dot_general | solution.py:152
  178.7 5.4 %convolution_convert_fusion.1 = bf16[512,6144]{1,0:T(8,128)(2,1)} fusion(bf16[512,512]{1,0:T(8,128)(2,1)S(1)} %fusion.14, bf16[1,512,6144]{2,1,0:T(8,128)(2,1)S(1)} %bitcast.130), kind=kOutput, calls=%fused_computation.2 | convolution fusion | flops 3224371200 | bytes 13107200 | tf_op jit(solution)/shard_map/dot_general | solution.py:154
  185.1 1.5 collective-permute-start.8
  186.5 20.2 %all-gather.5.cloned.1.call-done = bf16[512,6144]{1,0:T(8,128)(2,1)} async-done(((bf16[64,6144]{1,0:T(8,128)(2,1)}), bf16[512,6144]{1,0:T(8,128)(2,1)}) %all-gather.5.cloned.1.call-update) | async-done | bytes 6291472 | tf_op jit(solution)/shard_map/all_gather | solution.py:145
  206.7 7.6 %fusion.2 = f32[512,512]{1,0:T(8,128)S(1)} fusion(bf16[512,6144]{1,0:T(8,128)(2,1)} %all-gather.5.cloned.1.call-done, bf16[1,6144,512]{2,1,0:T(8,128)(2,1)} %param.22), kind=kOutput, calls=%fused_computation.6 | convolution fusion | flops 3221225472 | bytes 13631488 | tf_op jit(solution)/shard_map/dot_general | solution.py:152
  214.3 5.7 %fusion.6 = f32[512,512]{1,0:T(8,128)S(1)} fusion(bf16[512,6144]{1,0:T(8,128)(2,1)S(1)} %copy-done.6, bf16[1,6144,512]{2,1,0:T(8,128)(2,1)} %param.21), kind=kOutput, calls=%fused_computation.10 | convolution fusion | flops 3221225472 | bytes 13631488 | tf_op jit(solution)/shard_map/dot_general | solution.py:151
  220.1 5.4 %convolution_convert_fusion = bf16[512,6144]{1,0:T(8,128)(2,1)} fusion(bf16[1,512,6144]{2,1,0:T(8,128)(2,1)S(1)} %bitcast.132, f32[512,512]{1,0:T(8,128)S(1)} %fusion.2, f32[512,512]{1,0:T(8,128)S(1)} %fusion.6), kind=kOutput, calls=%fused_computation.1 | convolution fusion | flops 3225944064 | bytes 14680064 | tf_op jit(solution)/shard_map/dot_general | solution.py:154
  225.5 25.0 %reduce-scatter.3.cloned.1.call-done = bf16[64,6144]{1,0:T(8,128)(2,1)} async-done(((bf16[512,6144]{1,0:T(8,128)(2,1)}), bf16[64,6144]{1,0:T(8,128)(2,1)}) %reduce-scatter.3.cloned.1.call-update) | async-done | bytes 786448 | tf_op jit(solution)/shard_map/reduce_scatter | solution.py:155
  250.5 6.7 %all-to-all-start.3 = ((bf16[8,8,6144]{2,1,0:T(8,128)(2,1)}), bf16[8,8,6144]{2,1,0:T(8,128)(2,1)S(1)}, u32[]{:S(2)}, u32[]{:S(2)}) async-start(bf16[8,8,6144]{2,1,0:T(8,128)(2,1)} %bitcast.121), calls=%async_computation.4 | async-start | bytes 1572864 | tf_op jit(solution)/shard_map/all_to_all | solution.py:157
  257.4 37.6 %reduce-scatter.5.cloned.1.call-done = bf16[64,6144]{1,0:T(8,128)(2,1)} async-done(((bf16[512,6144]{1,0:T(8,128)(2,1)}), bf16[64,6144]{1,0:T(8,128)(2,1)}) %reduce-scatter.5.cloned.1.call-update) | async-done | bytes 786448 | tf_op jit(solution)/shard_map/reduce_scatter | solution.py:155
  295.1 6.7 %all-to-all-start.4 = ((bf16[8,8,6144]{2,1,0:T(8,128)(2,1)}), bf16[8,8,6144]{2,1,0:T(8,128)(2,1)}, u32[]{:S(2)}, u32[]{:S(2)}) async-start(bf16[8,8,6144]{2,1,0:T(8,128)(2,1)} %bitcast.122), calls=%async_computation.6 | async-start | bytes 1572864 | tf_op jit(solution)/shard_map/all_to_all | solution.py:157
  302.1 13.6 %all-to-all-done.4 = bf16[8,8,6144]{2,1,0:T(8,128)(2,1)} async-done(((bf16[8,8,6144]{2,1,0:T(8,128)(2,1)}), bf16[8,8,6144]{2,1,0:T(8,128)(2,1)}, u32[]{:S(2)}, u32[]{:S(2)}) %all-to-all-start.4) | async-done | bytes 786464 | tf_op jit(solution)/shard_map/all_to_all | solution.py:157
  315.8 1.2 pad_maximum_fusion
  320.3 9.6 %collective-permute-done.9 = bf16[32,6144]{1,0:T(8,128)(2,1)S(1)} collective-permute-done((bf16[32,6144]{1,0:T(8,128)(2,1)S(1)}, bf16[32,6144]{1,0:T(8,128)(2,1)S(1)}, u32[]{:S(2)}, u32[]{:S(2)}) %collective-permute-start.9) | collective-permute-done | bytes 393248 | tf_op jit(solution)/shard_map/ppermute | solution.py:173
  (114 shorter events, 17.5 us)
Async XLA Ops:
  6.5 295.3 %copy-start = (bf16[6144,8]{0,1:T(8,128)(2,1)S(1)}, bf16[6144,8]{0,1:T(8,128)(2,1)}, u32[]{:S(2)}) copy-start(bf16[6144,8]{0,1:T(8,128)(2,1)} %param.19) | copy-start | bytes 294916
  8.7 23.0 %collective-permute-start = (bf16[520,384]{0,1:T(8,128)(2,1)S(1)}, bf16[520,384]{0,1:T(8,128)(2,1)S(1)}, u32[]{:S(2)}, u32[]{:S(2)}) collective-permute-start(bf16[520,384]{0,1:T(8,128)(2,1)S(1)} %pad_maximum_fusion.1), channel_id=1, source_target_pairs={{0,32},{16,48},{32,64},{48,80},{64,96},{80,112},{96,0},{112,16},{1... | collective-permute-start | bytes 1198088 | tf_op jit(solution)/shard_map/ppermute | solution.py:74
  10.7 21.1 %collective-permute-start.1 = (bf16[520,384]{0,1:T(8,128)(2,1)S(1)}, bf16[520,384]{0,1:T(8,128)(2,1)S(1)}, u32[]{:S(2)}, u32[]{:S(2)}) collective-permute-start(bf16[520,384]{0,1:T(8,128)(2,1)S(1)} %pad_maximum_fusion.1), channel_id=1, source_target_pairs={{0,64},{16,80},{32,96},{48,112},{64,0},{80,16},{96,32},{112,48},{1... | collective-permute-start | bytes 1198088 | tf_op jit(solution)/shard_map/ppermute | solution.py:74
  11.8 23.2 %collective-permute-start.2 = (bf16[520,384]{0,1:T(8,128)(2,1)S(1)}, bf16[520,384]{0,1:T(8,128)(2,1)S(1)}, u32[]{:S(2)}, u32[]{:S(2)}) collective-permute-start(bf16[520,384]{0,1:T(8,128)(2,1)S(1)} %pad_maximum_fusion.1), channel_id=1, source_target_pairs={{0,96},{16,112},{32,0},{48,16},{64,32},{80,48},{96,64},{112,80},{1... | collective-permute-start | bytes 1198088 | tf_op jit(solution)/shard_map/ppermute | solution.py:74
  14.3 20.8 %collective-permute-start.3 = (bf16[520,384]{0,1:T(8,128)(2,1)S(1)}, bf16[520,384]{0,1:T(8,128)(2,1)S(1)}, u32[]{:S(2)}, u32[]{:S(2)}) collective-permute-start(bf16[520,384]{0,1:T(8,128)(2,1)S(1)} %pad_maximum_fusion.1), channel_id=1, source_target_pairs={{0,16},{16,0},{32,48},{48,32},{64,80},{80,64},{96,112},{112,96},{1... | collective-permute-start | bytes 1198088 | tf_op jit(solution)/shard_map/ppermute | solution.py:76
  31.7 3.6 %collective-permute-start.4 = (bf16[520,384]{0,1:T(8,128)(2,1)S(1)}, bf16[520,384]{0,1:T(8,128)(2,1)S(1)}, u32[]{:S(2)}, u32[]{:S(2)}) collective-permute-start(bf16[520,384]{0,1:T(8,128)(2,1)S(1)} %collective-permute-done), channel_id=1, source_target_pairs={{0,16},{16,0},{32,48},{48,32},{64,80},{80,64},{96,112},{112,96},{1... | collective-permute-start | bytes 1198088 | tf_op jit(solution)/shard_map/ppermute | solution.py:76
  31.7 3.6 %collective-permute-start.5 = (bf16[520,384]{0,1:T(8,128)(2,1)S(1)}, bf16[520,384]{0,1:T(8,128)(2,1)S(1)}, u32[]{:S(2)}, u32[]{:S(2)}) collective-permute-start(bf16[520,384]{0,1:T(8,128)(2,1)S(1)} %collective-permute-done.1), channel_id=1, source_target_pairs={{0,16},{16,0},{32,48},{48,32},{64,80},{80,64},{96,112},{112,96},{1... | collective-permute-start | bytes 1198088 | tf_op jit(solution)/shard_map/ppermute | solution.py:76
  35.0 1.9 collective-permute-start.6
  35.2 2.9 copy-start.8
  37.1 2.8 slice-start
  38.8 2.2 slice-start.1
  40.9 1.9 copy-start.3
  45.0 7.2 %copy-start.5 = (s32[32,2]{0,1:T(2,128)S(1)}, s32[32,2]{0,1:T(2,128)}, u32[]{:S(2)}) copy-start(s32[32,2]{0,1:T(2,128)} %param.20) | copy-start | bytes 772
  45.0 54.9 %copy-start.4 = (f32[6144]{0:T(1024)S(1)}, f32[6144]{0:T(1024)}, u32[]{:S(2)}) copy-start(f32[6144]{0:T(1024)} %param.18) | copy-start | bytes 73732
  45.0 53.7 %all-to-all-start = ((bf16[16,16,6144]{2,1,0:T(8,128)(2,1)}), bf16[16,16,6144]{2,1,0:T(8,128)(2,1)S(1)}, u32[]{:S(2)}, u32[]{:S(2)}) async-start(bf16[16,16,6144]{2,1,0:T(8,128)(2,1)} %bitcast.114), calls=%async_computation | async-start | bytes 6291456 | tf_op jit(solution)/shard_map/all_to_all | solution.py:110
  52.1 111.8 %all-gather.3.cloned.1.call-start = ((), (), s32[]{:S(2)}) async-start(), calls=%async_computation.7 | async-start | bytes 7077888 | tf_op jit(solution)/shard_map/all_gather | solution.py:145
  99.1 0.7 copy-start.1
  100.0 6.9 %collective-permute-start.7 = (bf16[16,6144]{1,0:T(8,128)(2,1)S(1)}, bf16[16,6144]{1,0:T(8,128)(2,1)S(1)}, u32[]{:S(2)}, u32[]{:S(2)}) collective-permute-start(bf16[16,6144]{1,0:T(8,128)(2,1)S(1)} %multiply_convert_fusion.2), channel_id=1, source_target_pairs={{0,1},{1,0},{2,3},{3,2},{4,5},{5,4},{6,7},{7,6},{8,9},{9,8},{10,11... | collective-permute-start | bytes 589832 | tf_op jit(solution)/shard_map/ppermute | solution.py:35
  126.6 80.1 %all-gather.5.cloned.1.call-start = ((), (), s32[]{:S(2)}) async-start(), calls=%async_computation.8 | async-start | bytes 7077888 | tf_op jit(solution)/shard_map/all_gather | solution.py:145
  141.3 109.2 %reduce-scatter.3.cloned.1.call-start = ((), (), s32[]{:S(2)}) async-start(), calls=%async_computation.9 | async-start | bytes 7077888 | tf_op jit(solution)/shard_map/reduce_scatter | solution.py:155
  163.9 8.3 %copy-start.7 = (bf16[512,6144]{1,0:T(8,128)(2,1)S(1)}, bf16[512,6144]{1,0:T(8,128)(2,1)}, u32[]{:S(2)}) copy-start(bf16[512,6144]{1,0:T(8,128)(2,1)} %all-gather.3.cloned.1.call-done) | copy-start | bytes 18874372
  163.9 14.7 %slice-start.2 = ((s8[6291456]{0:T(1024)(128)(4,1)}), s8[4194304]{0:T(1024)(128)(4,1)S(1)}, s32[]{:S(2)}) async-start(s8[6291456]{0:T(1024)(128)(4,1)} %bitcast.129), calls=%async_computation.13 | async-start | bytes 8388608
  172.2 6.4 %slice-start.3 = ((s8[6291456]{0:T(1024)(128)(4,1)}), s8[2097152]{0:T(1024)(128)(4,1)S(1)}, s32[]{:S(2)}) async-start(s8[6291456]{0:T(1024)(128)(4,1)} %bitcast.129), calls=%async_computation.14 | async-start | bytes 4194304
  184.1 1.0 copy-start.2
  184.1 111.0 %reduce-scatter.5.cloned.1.call-start = ((), (), s32[]{:S(2)}) async-start(), calls=%async_computation.10 | async-start | bytes 7077888 | tf_op jit(solution)/shard_map/reduce_scatter | solution.py:155
  185.1 21.6 %collective-permute-start.8 = (f32[16,6144]{1,0:T(8,128)S(1)}, f32[16,6144]{1,0:T(8,128)S(1)}, u32[]{:S(2)}, u32[]{:S(2)}) collective-permute-start(f32[16,6144]{1,0:T(8,128)S(1)} %copy-done.2), channel_id=1, source_target_pairs={{0,1},{1,0},{2,3},{3,2},{4,5},{5,4},{6,7},{7,6},{8,9},{9,8},{10,11... | collective-permute-start | bytes 1179656 | tf_op jit(solution)/shard_map/ppermute | solution.py:148
  206.7 7.6 %copy-start.6 = (bf16[512,6144]{1,0:T(8,128)(2,1)S(1)}, bf16[512,6144]{1,0:T(8,128)(2,1)}, u32[]{:S(2)}) copy-start(bf16[512,6144]{1,0:T(8,128)(2,1)} %all-gather.5.cloned.1.call-done) | copy-start | bytes 18874372
  206.7 13.4 %slice-start.4 = ((s8[6291456]{0:T(1024)(128)(4,1)}), s8[4194304]{0:T(1024)(128)(4,1)S(1)}, s32[]{:S(2)}) async-start(s8[6291456]{0:T(1024)(128)(4,1)} %bitcast.131), calls=%async_computation.15 | async-start | bytes 8388608
  214.3 5.8 %slice-start.5 = ((s8[6291456]{0:T(1024)(128)(4,1)}), s8[2097152]{0:T(1024)(128)(4,1)S(1)}, s32[]{:S(2)}) async-start(s8[6291456]{0:T(1024)(128)(4,1)} %bitcast.131), calls=%async_computation.16 | async-start | bytes 4194304
  250.5 44.6 %all-to-all-start.3 = ((bf16[8,8,6144]{2,1,0:T(8,128)(2,1)}), bf16[8,8,6144]{2,1,0:T(8,128)(2,1)S(1)}, u32[]{:S(2)}, u32[]{:S(2)}) async-start(bf16[8,8,6144]{2,1,0:T(8,128)(2,1)} %bitcast.121), calls=%async_computation.4 | async-start | bytes 1572864 | tf_op jit(solution)/shard_map/all_to_all | solution.py:157
  295.1 20.7 %all-to-all-start.4 = ((bf16[8,8,6144]{2,1,0:T(8,128)(2,1)}), bf16[8,8,6144]{2,1,0:T(8,128)(2,1)}, u32[]{:S(2)}, u32[]{:S(2)}) async-start(bf16[8,8,6144]{2,1,0:T(8,128)(2,1)} %bitcast.122), calls=%async_computation.6 | async-start | bytes 1572864 | tf_op jit(solution)/shard_map/all_to_all | solution.py:157
  319.2 10.8 %collective-permute-start.9 = (bf16[32,6144]{1,0:T(8,128)(2,1)S(1)}, bf16[32,6144]{1,0:T(8,128)(2,1)S(1)}, u32[]{:S(2)}, u32[]{:S(2)}) collective-permute-start(bf16[32,6144]{1,0:T(8,128)(2,1)S(1)} %fusion.26), channel_id=1, source_target_pairs={{0,1},{1,0},{2,3},{3,2},{4,5},{5,4},{6,7},{7,6},{8,9},{9,8},{10,11... | collective-permute-start | bytes 1179656 | tf_op jit(solution)/shard_map/ppermute | solution.py:173
Sparse Core Ops, SparseCore 0:
  126.7 37.2 all-gather.2
  165.6 41.0 all-gather.4
  209.1 41.3 reduce-scatter.2
  252.8 42.2 reduce-scatter.4
where the time goes:
time: 338 us
  waiting for transfers between devices  192 us (57%)
  matrix products  43 us (13%)
  blocking collectives  32.5 us (10%)
  starting transfers between devices  32.4 us (10%)
  between operations  18.6 us (6%)
  other arithmetic  9.42 us (3%)
  local copies, waits for them, and re-layouts  9.3 us (3%)
    reduce_scatter x2, waiting for transfers between devices, per_device(): part_rows = lax.psum_scatter(down, 'leaf', scatter_dimension=0, tiled=True)  62.6 us
    all_to_all x1, waiting for transfers between devices, per_device(): lax.all_to_all(term.reshape(group, share_rows, width), ('expert', 'tensor...  45.7 us
    all_gather x2, waiting for transfers between devices, per_device(): piece = lax.all_gather(arrived, 'leaf', axis=0, tiled=True)  42.6 us
    all_to_all x2, blocking collectives, per_device(): lax.all_to_all(outgoing[:, c * chunk_slots:(c + 1) * chunk_slots], 'exper...  32.5 us
    dot_general x2, matrix products, per_device(): up_v = jnp.dot(piece, w_up[0], preferred_element_type=jnp.float32)  14 us
    dot_general x2, matrix products, per_device(): gate_v = jnp.dot(piece, w_gate[0], preferred_element_type=jnp.float32)  14 us
    all_to_all x2, waiting for transfers between devices, per_device(): lax.all_to_all(part_rows.reshape(experts, chunk_slots, width), 'expert',...  13.6 us
    all_to_all x2, starting transfers between devices, per_device(): lax.all_to_all(part_rows.reshape(experts, chunk_slots, width), 'expert',...  13.4 us
  transfers between devices with their start and end apart: 17, of which 11 were waited for; matrix products, arithmetic and copies ran while one was open for 13% of the time, Pallas kernels for 0%

commit v1 on v0

--- a/solution.py
+++ b/solution.py
@@ -142,7 +142,8 @@
             concat_axis=0,
             tiled=True,
         ).reshape(-1, width)
-        piece = lax.all_gather(arrived, "leaf", axis=0, tiled=True)
+        copies = jnp.concatenate([arrived] * lax.axis_size("leaf"), axis=0)
+        piece = lax.all_to_all(copies, "leaf", 0, 0, tiled=True)
         if c == 0:
             piece, share = lax.optimization_barrier((piece, share))
             other_share = lax.ppermute(share, "tensor", perm=[(0, 1), (1, 0)])

time: 338 us -> 452 us (1.34)
  waiting for transfers between devices: 192 us -> 286 us
  starting transfers between devices: 32.4 us -> 47.8 us
  local copies, waits for them, and re-layouts: 9.3 us -> 24.6 us
  blocking collectives: 32.5 us -> 17.7 us
    all_to_all x0 -> x3, waiting for transfers between devices: none -> 165 us  [the longest x2 162 us: per_device(): piece = lax.all_to_all(copies, 'leaf', 0, 0, tiled=True)]
    all_gather x2 -> x0, waiting for transfers between devices: 42.6 us -> none  [per_device(): piece = lax.all_gather(arrived, 'leaf', axis=0, tiled=True)]
    reduce_scatter x2, waiting for transfers between devices: 62.6 us -> 33.7 us  [per_device(): part_rows = lax.psum_scatter(down, 'leaf', scatter_dimension=0, tiled=True)]
    all_to_all x0 -> x3, starting transfers between devices: none -> 16.1 us  [the longest x2 12.5 us: per_device(): piece = lax.all_to_all(copies, 'leaf', 0, 0, tiled=True)]
    all_to_all x2 -> x1, blocking collectives: 32.5 us -> 17.7 us  [per_device(): lax.all_to_all(outgoing[:, c * chunk_slots:(c + 1) * chunk_slots], 'exper...]
    unnamed x40 -> x54, local copies, waits for them, and re-layouts: 5.32 us -> 17.9 us
  transfers between devices with their start and end apart: 17 -> 18, of which waited for: 11 -> 11; matrix products, arithmetic and copies ran while one was open for 13% -> 9% of each run, Pallas kernels for 0% -> 0%
where the time goes in v1:
time: 452 us; the launch traced here: 451 us
  waiting for transfers between devices  286 us (63%)
  starting transfers between devices  47.8 us (11%)
  matrix products  46.1 us (10%)
  local copies, waits for them, and re-layouts  24.6 us (5%)
  between operations  18.9 us (4%)
  blocking collectives  17.7 us (4%)
  other arithmetic  9.42 us (2%)
    all_to_all x2, waiting for transfers between devices, per_device(): piece = lax.all_to_all(copies, 'leaf', 0, 0, tiled=True)  162 us
    all_to_all x1, waiting for transfers between devices, per_device(): lax.all_to_all(term.reshape(group, share_rows, width), ('expert', 'tensor...  45.8 us
    reduce_scatter x2, waiting for transfers between devices, per_device(): part_rows = lax.psum_scatter(down, 'leaf', scatter_dimension=0, tiled=True)  33.7 us
    unnamed x54, local copies, waits for them, and re-layouts  17.9 us
    all_to_all x1, blocking collectives, per_device(): lax.all_to_all(outgoing[:, c * chunk_slots:(c + 1) * chunk_slots], 'exper...  17.7 us
    dot_general x2, matrix products, per_device(): up_v = jnp.dot(piece, w_up[0], preferred_element_type=jnp.float32)  15.9 us
    dot_general x2, matrix products, per_device(): gate_v = jnp.dot(piece, w_gate[0], preferred_element_type=jnp.float32)  15.2 us
    all_to_all x2, waiting for transfers between devices, per_device(): lax.all_to_all(part_rows.reshape(experts, chunk_slots, width), 'expert',...  13.7 us
  transfers between devices with their start and end apart: 18, of which 11 were waited for; matrix products, arithmetic and copies ran while one was open for 9% of the time, Pallas kernels for 0%

profile of v1, /device:TPU:32, one launch (start us, length us, event | category | flops | bytes accessed | tf_op | source)
XLA Modules:
  0.0 451.0 jit_solution(8198249437738042762)
XLA Ops:
  6.5 1.2 copy.74
  8.7 2.0 collective-permute-start
  11.8 2.5 collective-permute-start.2
  21.9 9.8 %collective-permute-done = bf16[520,384]{0,1:T(8,128)(2,1)S(1)} collective-permute-done((bf16[520,384]{0,1:T(8,128)(2,1)S(1)}, bf16[520,384]{0,1:T(8,128)(2,1)S(1)}, u32[]{:S(2)}, u32[]{:S(2)}) %collective-permute-start) | collective-permute-done | bytes 399392 | tf_op jit(solution)/shard_map/ppermute | solution.py:74
  32.3 2.7 collective-permute-done.2
  35.4 1.5 collective-permute-done.6
  40.9 1.8 fusion.50
  42.9 2.1 convert_element_type.89
  45.0 7.2 %all-to-all-start = ((bf16[16,16,6144]{2,1,0:T(8,128)(2,1)}), bf16[16,16,6144]{2,1,0:T(8,128)(2,1)S(1)}, u32[]{:S(2)}, u32[]{:S(2)}) async-start(bf16[16,16,6144]{2,1,0:T(8,128)(2,1)} %bitcast.134), calls=%async_computation | async-start | bytes 6291456 | tf_op jit(solution)/shard_map/all_to_all | solution.py:110
  52.9 45.8 %all-to-all-done = bf16[16,16,6144]{2,1,0:T(8,128)(2,1)S(1)} async-done(((bf16[16,16,6144]{2,1,0:T(8,128)(2,1)}), bf16[16,16,6144]{2,1,0:T(8,128)(2,1)S(1)}, u32[]{:S(2)}, u32[]{:S(2)}) %all-to-all-start) | async-done | bytes 3145760 | tf_op jit(solution)/shard_map/all_to_all | solution.py:110
  100.0 2.8 collective-permute-start.7
  102.8 4.0 collective-permute-done.7
  109.6 17.7 %all_to_all.49 = bf16[8,8,6144]{2,1,0:T(8,128)(2,1)S(1)} all-to-all(bf16[8,8,6144]{2,1,0:T(8,128)(2,1)S(1)} %get-tuple-element.19), channel_id=1, replica_groups=mesh['leaf'=8,'expert'=8,'tensor'=2] {'expert'}, dimensions={0} | all-to-all | bytes 1572864 | tf_op jit(solution)/shard_map/all_to_all | solution.py:138
  127.3 3.5 all-to-all-start.3
  138.6 3.0 all-to-all-done.3
  141.6 6.2 %all-to-all-start.2 = ((bf16[8,64,6144]{2,1,0:T(8,128)(2,1)}), bf16[8,64,6144]{2,1,0:T(8,128)(2,1)}, u32[]{:S(2)}, u32[]{:S(2)}) async-start(bf16[8,64,6144]{2,1,0:T(8,128)(2,1)} %bitcast.21), calls=%async_computation.2 | async-start | bytes 12582912 | tf_op jit(solution)/shard_map/all_to_all | solution.py:146
  152.6 66.0 %all-to-all-done.2 = bf16[8,64,6144]{2,1,0:T(8,128)(2,1)} async-done(((bf16[8,64,6144]{2,1,0:T(8,128)(2,1)}), bf16[8,64,6144]{2,1,0:T(8,128)(2,1)}, u32[]{:S(2)}, u32[]{:S(2)}) %all-to-all-start.2) | async-done | bytes 6291488 | tf_op jit(solution)/shard_map/all_to_all | solution.py:146
  218.6 7.6 %fusion.8 = f32[512,512]{1,0:T(8,128)S(1)} fusion(bf16[512,6144]{1,0:T(8,128)(2,1)} %bitcast.22, bf16[1,6144,512]{2,1,0:T(8,128)(2,1)} %param.21), kind=kOutput, calls=%fused_computation.12 | convolution fusion | flops 3221225472 | bytes 13631488 | tf_op jit(solution)/shard_map/dot_general | solution.py:152
  226.2 8.2 %fusion.14 = bf16[512,512]{1,0:T(8,128)(2,1)S(1)} fusion(bf16[512,6144]{1,0:T(8,128)(2,1)} %bitcast.22, bf16[1,6144,512]{2,1,0:T(8,128)(2,1)} %param.22, f32[512,512]{1,0:T(8,128)S(1)} %fusion.8), kind=kOutput, calls=%fused_computation.22 | convolution fusion | flops 3222798336 | bytes 14155776 | tf_op jit(solution)/shard_map/dot_general | solution.py:153
  234.5 5.4 %convolution_convert_fusion.1 = bf16[512,6144]{1,0:T(8,128)(2,1)} fusion(bf16[512,512]{1,0:T(8,128)(2,1)S(1)} %fusion.14, bf16[1,512,6144]{2,1,0:T(8,128)(2,1)S(1)} %bitcast.148), kind=kOutput, calls=%fused_computation.2 | convolution fusion | flops 3224371200 | bytes 13107200 | tf_op jit(solution)/shard_map/dot_general | solution.py:155
  242.8 6.4 %all-to-all-start.4 = ((bf16[8,64,6144]{2,1,0:T(8,128)(2,1)}), bf16[8,64,6144]{2,1,0:T(8,128)(2,1)}, u32[]{:S(2)}, u32[]{:S(2)}) async-start(bf16[8,64,6144]{2,1,0:T(8,128)(2,1)} %bitcast.24), calls=%async_computation.4 | async-start | bytes 12582912 | tf_op jit(solution)/shard_map/all_to_all | solution.py:146
  249.2 1.2 collective-permute-start.8
  250.3 96.4 %all-to-all-done.4 = bf16[8,64,6144]{2,1,0:T(8,128)(2,1)} async-done(((bf16[8,64,6144]{2,1,0:T(8,128)(2,1)}), bf16[8,64,6144]{2,1,0:T(8,128)(2,1)}, u32[]{:S(2)}, u32[]{:S(2)}) %all-to-all-start.4) | async-done | bytes 6291488 | tf_op jit(solution)/shard_map/all_to_all | solution.py:146
  346.8 7.6 %fusion.2 = f32[512,512]{1,0:T(8,128)S(1)} fusion(bf16[512,6144]{1,0:T(8,128)(2,1)} %bitcast.25, bf16[1,6144,512]{2,1,0:T(8,128)(2,1)} %param.22), kind=kOutput, calls=%fused_computation.6 | convolution fusion | flops 3221225472 | bytes 13631488 | tf_op jit(solution)/shard_map/dot_general | solution.py:153
  354.4 7.6 %fusion.6 = f32[512,512]{1,0:T(8,128)S(1)} fusion(bf16[512,6144]{1,0:T(8,128)(2,1)} %bitcast.25, bf16[1,6144,512]{2,1,0:T(8,128)(2,1)} %param.21), kind=kOutput, calls=%fused_computation.10 | convolution fusion | flops 3221225472 | bytes 13631488 | tf_op jit(solution)/shard_map/dot_general | solution.py:152
  362.1 5.4 %convolution_convert_fusion = bf16[512,6144]{1,0:T(8,128)(2,1)} fusion(bf16[1,512,6144]{2,1,0:T(8,128)(2,1)S(1)} %bitcast.150, f32[512,512]{1,0:T(8,128)S(1)} %fusion.2, f32[512,512]{1,0:T(8,128)S(1)} %fusion.6), kind=kOutput, calls=%fused_computation.1 | convolution fusion | flops 3225944064 | bytes 14680064 | tf_op jit(solution)/shard_map/dot_general | solution.py:155
  367.5 6.7 %all-to-all-start.5 = ((bf16[8,8,6144]{2,1,0:T(8,128)(2,1)}), bf16[8,8,6144]{2,1,0:T(8,128)(2,1)S(1)}, u32[]{:S(2)}, u32[]{:S(2)}) async-start(bf16[8,8,6144]{2,1,0:T(8,128)(2,1)} %bitcast.139), calls=%async_computation.6 | async-start | bytes 1572864 | tf_op jit(solution)/shard_map/all_to_all | solution.py:158
  374.4 33.7 %reduce-scatter.5.cloned.1.call-done = bf16[64,6144]{1,0:T(8,128)(2,1)} async-done(((bf16[512,6144]{1,0:T(8,128)(2,1)}), bf16[64,6144]{1,0:T(8,128)(2,1)}) %reduce-scatter.5.cloned.1.call-update) | async-done | bytes 786448 | tf_op jit(solution)/shard_map/reduce_scatter | solution.py:156
  408.1 6.7 %all-to-all-start.6 = ((bf16[8,8,6144]{2,1,0:T(8,128)(2,1)}), bf16[8,8,6144]{2,1,0:T(8,128)(2,1)}, u32[]{:S(2)}, u32[]{:S(2)}) async-start(bf16[8,8,6144]{2,1,0:T(8,128)(2,1)} %bitcast.140), calls=%async_computation.8 | async-start | bytes 1572864 | tf_op jit(solution)/shard_map/all_to_all | solution.py:158
  415.1 13.7 %all-to-all-done.6 = bf16[8,8,6144]{2,1,0:T(8,128)(2,1)} async-done(((bf16[8,8,6144]{2,1,0:T(8,128)(2,1)}), bf16[8,8,6144]{2,1,0:T(8,128)(2,1)}, u32[]{:S(2)}, u32[]{:S(2)}) %all-to-all-start.6) | async-done | bytes 786464 | tf_op jit(solution)/shard_map/all_to_all | solution.py:158
  428.8 1.2 pad_maximum_fusion
  433.4 9.7 %collective-permute-done.9 = bf16[32,6144]{1,0:T(8,128)(2,1)S(1)} collective-permute-done((bf16[32,6144]{1,0:T(8,128)(2,1)S(1)}, bf16[32,6144]{1,0:T(8,128)(2,1)S(1)}, u32[]{:S(2)}, u32[]{:S(2)}) %collective-permute-start.9) | collective-permute-done | bytes 393248 | tf_op jit(solution)/shard_map/ppermute | solution.py:174
  (129 shorter events, 34.7 us)
Async XLA Ops:
  6.5 408.3 %copy-start = (bf16[6144,8]{0,1:T(8,128)(2,1)S(1)}, bf16[6144,8]{0,1:T(8,128)(2,1)}, u32[]{:S(2)}) copy-start(bf16[6144,8]{0,1:T(8,128)(2,1)} %param.19) | copy-start | bytes 294916
  8.7 23.0 %collective-permute-start = (bf16[520,384]{0,1:T(8,128)(2,1)S(1)}, bf16[520,384]{0,1:T(8,128)(2,1)S(1)}, u32[]{:S(2)}, u32[]{:S(2)}) collective-permute-start(bf16[520,384]{0,1:T(8,128)(2,1)S(1)} %pad_maximum_fusion.1), channel_id=1, source_target_pairs={{0,32},{16,48},{32,64},{48,80},{64,96},{80,112},{96,0},{112,16},{1... | collective-permute-start | bytes 1198088 | tf_op jit(solution)/shard_map/ppermute | solution.py:74
  10.7 21.1 %collective-permute-start.1 = (bf16[520,384]{0,1:T(8,128)(2,1)S(1)}, bf16[520,384]{0,1:T(8,128)(2,1)S(1)}, u32[]{:S(2)}, u32[]{:S(2)}) collective-permute-start(bf16[520,384]{0,1:T(8,128)(2,1)S(1)} %pad_maximum_fusion.1), channel_id=1, source_target_pairs={{0,64},{16,80},{32,96},{48,112},{64,0},{80,16},{96,32},{112,48},{1... | collective-permute-start | bytes 1198088 | tf_op jit(solution)/shard_map/ppermute | solution.py:74
  11.8 23.2 %collective-permute-start.2 = (bf16[520,384]{0,1:T(8,128)(2,1)S(1)}, bf16[520,384]{0,1:T(8,128)(2,1)S(1)}, u32[]{:S(2)}, u32[]{:S(2)}) collective-permute-start(bf16[520,384]{0,1:T(8,128)(2,1)S(1)} %pad_maximum_fusion.1), channel_id=1, source_target_pairs={{0,96},{16,112},{32,0},{48,16},{64,32},{80,48},{96,64},{112,80},{1... | collective-permute-start | bytes 1198088 | tf_op jit(solution)/shard_map/ppermute | solution.py:74
  14.3 20.8 %collective-permute-start.3 = (bf16[520,384]{0,1:T(8,128)(2,1)S(1)}, bf16[520,384]{0,1:T(8,128)(2,1)S(1)}, u32[]{:S(2)}, u32[]{:S(2)}) collective-permute-start(bf16[520,384]{0,1:T(8,128)(2,1)S(1)} %pad_maximum_fusion.1), channel_id=1, source_target_pairs={{0,16},{16,0},{32,48},{48,32},{64,80},{80,64},{96,112},{112,96},{1... | collective-permute-start | bytes 1198088 | tf_op jit(solution)/shard_map/ppermute | solution.py:76
  18.4 19.7 %copy-start.8 = (f32[3,16]{1,0:T(4,128)S(1)}, f32[3,16]{1,0:T(4,128)}, u32[]{:S(2)}) copy-start(f32[3,16]{1,0:T(4,128)} %param.16) | copy-start | bytes 580
  31.7 3.5 collective-permute-start.4
  31.7 3.6 collective-permute-start.5
  35.0 1.9 collective-permute-start.6
  37.1 2.8 slice-start
  38.8 2.2 slice-start.1
  39.9 2.9 copy-start.3
  42.9 9.2 %copy-start.7 = (s32[32,2]{0,1:T(2,128)S(1)}, s32[32,2]{0,1:T(2,128)}, u32[]{:S(2)}) copy-start(s32[32,2]{0,1:T(2,128)} %param.20) | copy-start | bytes 772
  45.0 54.9 %copy-start.6 = (f32[6144]{0:T(1024)S(1)}, f32[6144]{0:T(1024)}, u32[]{:S(2)}) copy-start(f32[6144]{0:T(1024)} %param.18) | copy-start | bytes 73732
  45.0 53.7 %all-to-all-start = ((bf16[16,16,6144]{2,1,0:T(8,128)(2,1)}), bf16[16,16,6144]{2,1,0:T(8,128)(2,1)S(1)}, u32[]{:S(2)}, u32[]{:S(2)}) async-start(bf16[16,16,6144]{2,1,0:T(8,128)(2,1)} %bitcast.134), calls=%async_computation | async-start | bytes 6291456 | tf_op jit(solution)/shard_map/all_to_all | solution.py:110
  100.0 6.9 %collective-permute-start.7 = (bf16[16,6144]{1,0:T(8,128)(2,1)S(1)}, bf16[16,6144]{1,0:T(8,128)(2,1)S(1)}, u32[]{:S(2)}, u32[]{:S(2)}) collective-permute-start(bf16[16,6144]{1,0:T(8,128)(2,1)S(1)} %multiply_convert_fusion.2), channel_id=1, source_target_pairs={{0,1},{1,0},{2,3},{3,2},{4,5},{5,4},{6,7},{7,6},{8,9},{9,8},{10,11... | collective-permute-start | bytes 589832 | tf_op jit(solution)/shard_map/ppermute | solution.py:35
  127.3 14.3 %all-to-all-start.3 = ((bf16[8,8,6144]{2,1,0:T(8,128)(2,1)}), bf16[8,8,6144]{2,1,0:T(8,128)(2,1)S(1)}, u32[]{:S(2)}, u32[]{:S(2)}) async-start(bf16[8,8,6144]{2,1,0:T(8,128)(2,1)} %get-tuple-element.20), calls=%async_computation.3 | async-start | bytes 1572864 | tf_op jit(solution)/shard_map/all_to_all | solution.py:138
  141.6 77.0 %all-to-all-start.2 = ((bf16[8,64,6144]{2,1,0:T(8,128)(2,1)}), bf16[8,64,6144]{2,1,0:T(8,128)(2,1)}, u32[]{:S(2)}, u32[]{:S(2)}) async-start(bf16[8,64,6144]{2,1,0:T(8,128)(2,1)} %bitcast.21), calls=%async_computation.2 | async-start | bytes 12582912 | tf_op jit(solution)/shard_map/all_to_all | solution.py:146
  147.8 219.7 %reduce-scatter.3.cloned.1.call-start = ((), (), s32[]{:S(2)}) async-start(), calls=%async_computation.9 | async-start | bytes 7077888 | tf_op jit(solution)/shard_map/reduce_scatter | solution.py:156
  218.6 15.9 %slice-start.2 = ((s8[6291456]{0:T(1024)(128)(4,1)}), s8[4194304]{0:T(1024)(128)(4,1)S(1)}, s32[]{:S(2)}) async-start(s8[6291456]{0:T(1024)(128)(4,1)} %bitcast.147), calls=%async_computation.13 | async-start | bytes 8388608
  226.2 8.3 %slice-start.3 = ((s8[6291456]{0:T(1024)(128)(4,1)}), s8[2097152]{0:T(1024)(128)(4,1)S(1)}, s32[]{:S(2)}) async-start(s8[6291456]{0:T(1024)(128)(4,1)} %bitcast.147), calls=%async_computation.14 | async-start | bytes 4194304
  242.8 6.4 %copy-start.2 = (f32[16,6144]{1,0:T(8,128)S(1)}, f32[16,6144]{1,0:T(8,128)}, u32[]{:S(2)}) copy-start(f32[16,6144]{1,0:T(8,128)} %copy-done.1) | copy-start | bytes 1179652
  242.8 104.0 %all-to-all-start.4 = ((bf16[8,64,6144]{2,1,0:T(8,128)(2,1)}), bf16[8,64,6144]{2,1,0:T(8,128)(2,1)}, u32[]{:S(2)}, u32[]{:S(2)}) async-start(bf16[8,64,6144]{2,1,0:T(8,128)(2,1)} %bitcast.24), calls=%async_computation.4 | async-start | bytes 12582912 | tf_op jit(solution)/shard_map/all_to_all | solution.py:146
  249.2 158.9 %reduce-scatter.5.cloned.1.call-start = ((), (), s32[]{:S(2)}) async-start(), calls=%async_computation.10 | async-start | bytes 7077888 | tf_op jit(solution)/shard_map/reduce_scatter | solution.py:156
  249.2 97.6 %collective-permute-start.8 = (f32[16,6144]{1,0:T(8,128)S(1)}, f32[16,6144]{1,0:T(8,128)S(1)}, u32[]{:S(2)}, u32[]{:S(2)}) collective-permute-start(f32[16,6144]{1,0:T(8,128)S(1)} %copy-done.2), channel_id=1, source_target_pairs={{0,1},{1,0},{2,3},{3,2},{4,5},{5,4},{6,7},{7,6},{8,9},{9,8},{10,11... | collective-permute-start | bytes 1179656 | tf_op jit(solution)/shard_map/ppermute | solution.py:149
  346.8 7.6 %copy-start.4 = (f32[16,6144]{1,0:T(8,128)}, f32[16,6144]{1,0:T(8,128)S(1)}, u32[]{:S(2)}) copy-start(f32[16,6144]{1,0:T(8,128)S(1)} %collective-permute-done.8) | copy-start | bytes 1179652
  346.8 15.3 %slice-start.4 = ((s8[6291456]{0:T(1024)(128)(4,1)}), s8[4194304]{0:T(1024)(128)(4,1)S(1)}, s32[]{:S(2)}) async-start(s8[6291456]{0:T(1024)(128)(4,1)} %bitcast.149), calls=%async_computation.15 | async-start | bytes 8388608
  354.4 7.6 %slice-start.5 = ((s8[6291456]{0:T(1024)(128)(4,1)}), s8[2097152]{0:T(1024)(128)(4,1)S(1)}, s32[]{:S(2)}) async-start(s8[6291456]{0:T(1024)(128)(4,1)} %bitcast.149), calls=%async_computation.16 | async-start | bytes 4194304
  367.5 40.6 %all-to-all-start.5 = ((bf16[8,8,6144]{2,1,0:T(8,128)(2,1)}), bf16[8,8,6144]{2,1,0:T(8,128)(2,1)S(1)}, u32[]{:S(2)}, u32[]{:S(2)}) async-start(bf16[8,8,6144]{2,1,0:T(8,128)(2,1)} %bitcast.139), calls=%async_computation.6 | async-start | bytes 1572864 | tf_op jit(solution)/shard_map/all_to_all | solution.py:158
  408.1 20.7 %all-to-all-start.6 = ((bf16[8,8,6144]{2,1,0:T(8,128)(2,1)}), bf16[8,8,6144]{2,1,0:T(8,128)(2,1)}, u32[]{:S(2)}, u32[]{:S(2)}) async-start(bf16[8,8,6144]{2,1,0:T(8,128)(2,1)} %bitcast.140), calls=%async_computation.8 | async-start | bytes 1572864 | tf_op jit(solution)/shard_map/all_to_all | solution.py:158
  430.0 3.3 copy-start.5
  432.3 10.8 %collective-permute-start.9 = (bf16[32,6144]{1,0:T(8,128)(2,1)S(1)}, bf16[32,6144]{1,0:T(8,128)(2,1)S(1)}, u32[]{:S(2)}, u32[]{:S(2)}) collective-permute-start(bf16[32,6144]{1,0:T(8,128)(2,1)S(1)} %fusion.26), channel_id=1, source_target_pairs={{0,1},{1,0},{2,3},{3,2},{4,5},{5,4},{6,7},{7,6},{8,9},{9,8},{10,11... | collective-permute-start | bytes 1179656 | tf_op jit(solution)/shard_map/ppermute | solution.py:174
  (1 other events, 0.7 us)
Sparse Core Ops, SparseCore 0:
  240.1 90.7 reduce-scatter.2
  367.6 40.4 reduce-scatter.4
